TPU v7x, 256 devices: a whole 4x4x8 slice. The times are simulated.
256 devices in a mesh: orient: 16 (over y, x_lo, core), strip: 16 (over x_hi, z).
Axes of the slice: x: 4 (x_hi: 2, x_lo: 2; x = x_hi * 2 + x_lo), y: 4, z: 8, core: 2. Of those that a mesh axis runs over, the one named last changes fastest.
Arguments:
- inflow_field: bfloat16 [32, 8, 128, 512], P('orient', None, 'strip'), may hold values from -6 to 6
- kernel_one: bfloat16 [32, 9, 8, 8], replicated, may hold values from -0.125 to 0.125
- kernel_two: bfloat16 [32, 9, 8, 8], replicated, may hold values from -0.125 to 0.125
- turbine_mask: int32 [128, 512], P('strip'), may hold values 0 or 1
- wind_sector: int32 [1], replicated, may hold values from 0 to 31
- wake_cotangent: bfloat16 [32, 8, 128, 512], P('orient', None, 'strip'), may hold values from -6 to 6
Outputs:
- wake_out: bfloat16 [32, 8, 128, 512], P('orient', None, 'strip')
- kernel_grad_one: float32 [32, 9, 8, 8], replicated
- kernel_grad_two: float32 [32, 9, 8, 8], replicated
Inputs may be any that keep to these rules, and one draw needn't show every extreme that they name: `wind_sector`: names one element of the group.
All inputs are finite; a program needn't handle non-finite values. No bound on the sum of `turbine_mask` on one device may be relied on, other than what follows from the above.
Results may differ from a plain program's by a relative error of at most 0.0051.
Values may be sent and summed in bfloat16 or wider, within the bound.
No kernel may reach another device: no remote copies, remote signals or barrier semaphores. Data moves between devices by JAX's collectives and lax.ppermute only.
A program may use at most 128 MiB of HBM per device.

v0:
```python
import math
import jax
import jax.numpy as jnp
from jax import lax
from jax.sharding import PartitionSpec as P

G = 32
OFFSETS = ((0, 0), (0, 1), (0, 2), (1, 0), (1, 1), (1, 2), (2, 0), (2, 1), (2, 2))


def with_halo(shard, sides, width):
    for axis, dim in sides:
        count, length = (lax.axis_size(axis), shard.shape[dim])
        up = [(i, (i + 1) % count) for i in range(count - 1)]
        down = [(j, i) for i, j in up]
        last = lax.slice_in_dim(shard, length - width, length, axis=dim)
        first = lax.slice_in_dim(shard, 0, width, axis=dim)
        before = lax.ppermute(last, axis, up)
        after = lax.ppermute(first, axis, down)
        shard = jnp.concatenate([before, shard, after], axis=dim)
    return shard


def relative(row_ids, col_ids, sector):
    halfway = G // 2
    row_rot = row_ids % halfway
    row_ref = row_ids // halfway
    col_rot = col_ids % halfway
    col_ref = col_ids // halfway
    sec_rot = sector % halfway
    sec_ref = sector // halfway
    moved_rot = (sec_rot + (1 - 2 * sec_ref) * col_rot) % halfway
    moved_ref = (sec_ref + col_ref) % 2
    inverse_rot = jnp.where(row_ref == 0, (halfway - row_rot) % halfway, row_rot)
    result_rot = (inverse_rot + (1 - 2 * row_ref) * moved_rot) % halfway
    result_ref = (row_ref + moved_ref) % 2
    return result_ref * halfway + result_rot


def kernel_block(kernel, row_ids, col_ids, sector):
    channels = kernel.shape[2]
    tap_count = kernel.shape[1]
    relation = relative(row_ids[:, None], col_ids[None, :], sector).reshape(-1)
    onehot = (relation[:, None] == jnp.arange(G, dtype=jnp.int32)[None, :]).astype(jnp.bfloat16)
    picked = jnp.dot(onehot, kernel.reshape(G, -1), preferred_element_type=jnp.float32)
    picked = picked.reshape(row_ids.shape[0], col_ids.shape[0], tap_count, channels, channels)
    picked = picked.transpose(2, 0, 3, 1, 4)
    return picked.reshape(
        tap_count, row_ids.shape[0] * channels, col_ids.shape[0] * channels
    ).astype(jnp.bfloat16)


def fold_kernel(partial_grad, row_ids, col_ids, sector):
    tap_count = partial_grad.shape[0]
    channels = partial_grad.shape[1] // row_ids.shape[0]
    relation = relative(row_ids[:, None], col_ids[None, :], sector).reshape(-1)
    onehot = (relation[:, None] == jnp.arange(G, dtype=jnp.int32)[None, :]).astype(jnp.float32)
    arranged = partial_grad.reshape(
        tap_count, row_ids.shape[0], channels, col_ids.shape[0], channels
    )
    arranged = arranged.transpose(1, 3, 0, 2, 4).reshape(relation.shape[0], -1)
    folded = jnp.dot(
        onehot.T, arranged, precision=lax.Precision.HIGHEST, preferred_element_type=jnp.float32
    )
    return folded.reshape(G, tap_count, channels, channels)


def place_forward(mixed_taps, height, extent):
    padded = jnp.pad(mixed_taps, ((0, 0), (0, 0), (0, 0), (1, 1)))
    summed = jnp.zeros((mixed_taps.shape[1], height, extent), jnp.float32)
    for tap_index, (row_shift, col_shift) in enumerate(OFFSETS):
        summed = (
            summed
            + padded[tap_index, :, row_shift : row_shift + height, col_shift : col_shift + extent]
        )
    return summed


def place_backward(mixed_taps, height, extent):
    padded = jnp.pad(mixed_taps, ((0, 0), (0, 0), (0, 0), (1, 1)))
    summed = jnp.zeros((mixed_taps.shape[1], height, extent), jnp.float32)
    for tap_index, (row_shift, col_shift) in enumerate(OFFSETS):
        summed = (
            summed
            + padded[
                tap_index,
                :,
                2 - row_shift : 2 - row_shift + height,
                2 - col_shift : 2 - col_shift + extent,
            ]
        )
    return summed


def layer_forward(source, weights_row):
    tap_count, local_width, full_width = weights_row.shape
    height, extent = (source.shape[1], source.shape[2])
    matrix = weights_row.reshape(tap_count * local_width, full_width)
    widened = with_halo(source, (("strip", 1),), 1)
    gathered = lax.all_gather(widened, "orient", axis=0, tiled=True)
    mixed_taps = jnp.dot(
        matrix, gathered.reshape(full_width, -1), preferred_element_type=jnp.float32
    )
    mixed_taps = mixed_taps.reshape(tap_count, local_width, gathered.shape[1], extent)
    center = gathered[:, 1 : height + 1]
    return (place_forward(mixed_taps, height, extent), center)


def rim_rows(gradient):
    return with_halo(gradient, (("strip", 1),), 1)


def weight_grad(cot_rows, center):
    height, extent = (center.shape[1], center.shape[2])
    padded = jnp.pad(cot_rows, ((0, 0), (0, 0), (1, 1)))
    flat_center = center.reshape(center.shape[0], -1)
    pieces = []
    for row_shift, col_shift in OFFSETS:
        window = padded[
            :, 2 - row_shift : 2 - row_shift + height, 2 - col_shift : 2 - col_shift + extent
        ]
        window = window.reshape(cot_rows.shape[0], -1)
        pieces.append(
            lax.dot_general(
                window, flat_center, (((1,), (1,)), ((), ())), preferred_element_type=jnp.float32
            )
        )
    return jnp.stack(pieces, 0)


def shards(inflow_field, kernel_one, kernel_two, turbine_mask, wind_sector, wake_cotangent):
    groups, channels, height, extent = inflow_field.shape
    local_width = groups * channels
    sector = wind_sector[0]
    neutral = jnp.int32(0)
    all_groups = jnp.arange(G, dtype=jnp.int32)
    scale_factor = 1.0 / math.sqrt(G * height * lax.axis_size("strip") * extent)
    first_group = lax.axis_index("orient") * groups
    my_groups = first_group + jnp.arange(groups, dtype=jnp.int32)
    row_one = kernel_block(kernel_one, my_groups, all_groups, sector)
    row_two = kernel_block(kernel_two, my_groups, all_groups, neutral)
    open_cells = (1 - turbine_mask).astype(jnp.float32)
    source = inflow_field.reshape(local_width, height, extent)
    first_pre, first_center = layer_forward(source, row_one)
    sigmoid_one = jax.nn.sigmoid(first_pre)
    hidden = (first_pre * sigmoid_one * open_cells).astype(jnp.bfloat16)
    second_pre, second_center = layer_forward(hidden, row_two)
    wake_out = second_pre.astype(jnp.bfloat16).reshape(groups, channels, height, extent)
    cotangent = wake_cotangent.reshape(local_width, height, extent)
    cot_two = rim_rows(cotangent)
    grad_two = weight_grad(cot_two, second_center)
    rows_turned = row_two.transpose(0, 2, 1)
    mixed_taps = jnp.dot(
        rows_turned.reshape(9 * (local_width * lax.axis_size("orient")), local_width),
        cot_two.reshape(local_width, -1),
        preferred_element_type=jnp.float32,
    )
    mixed_taps = mixed_taps.reshape(9, local_width * lax.axis_size("orient"), height + 2, extent)
    back_grad = lax.psum_scatter(
        place_backward(mixed_taps, height, extent), "orient", scatter_dimension=0, tiled=True
    )
    first_grad = (
        back_grad * open_cells * sigmoid_one * (1.0 + first_pre * (1.0 - sigmoid_one))
    ).astype(jnp.bfloat16)
    cot_one = rim_rows(first_grad)
    grad_one = weight_grad(cot_one, first_center)
    share_one = fold_kernel(grad_one, my_groups, all_groups, sector) * scale_factor
    share_two = fold_kernel(grad_two, my_groups, all_groups, neutral) * scale_factor
    summed_one, summed_two = lax.psum((share_one, share_two), ("orient", "strip"))
    return (wake_out, summed_one, summed_two)


def solution(mesh):
    return jax.shard_map(
        shards,
        mesh=mesh,
        in_specs=(
            P("orient", None, "strip", None),
            P(),
            P(),
            P("strip", None),
            P(),
            P("orient", None, "strip", None),
        ),
        out_specs=(P("orient", None, "strip", None), P(), P()),
        check_vma=False,
    )
```

profile of v0, /device:TPU:2, one launch (start us, length us, event | category | flops | bytes accessed | tf_op | source)
XLA Modules:
  0.0 480.0 jit_solution(5787390711143419611)
XLA Ops:
  8.2 3.8 collective-permute-start
  13.4 4.2 collective-permute-done.1
  19.4 3.8 collective-permute-start.4
  27.4 1.8 convert_element_type.51
  29.9 18.7 %fusion.60 = f32[9,256,10,512]{3,1,2,0:T(8,128)} fusion(bf16[9,16,256]{2,1,0:T(8,128)(2,1)S(1)} %convert_element_type.51, bf16[10,2,8,512]{3,2,1,0:T(8,128)(2,1)S(1)} %get-tuple-element.21), kind=kOutput, calls=%fused_computation.112 | convolution fusion | flops 377487360 | bytes 47423488 | tf_op jit(solution)/shard_map/dot_general | solution.py:153
  48.6 17.5 %fusion.8 = f32[256,8,512]{2,0,1:T(8,128)} fusion(f32[9,256,10,512]{3,1,2,0:T(8,128)} %fusion.60), kind=kLoop, calls=%fused_computation.26 | loop fusion | flops 8388608 | bytes 63963136 | tf_op jit(solution)/shard_map/add | solution.py:84
  68.1 1.7 reshape.552
  69.9 4.4 copy.36
  74.3 2.7 fusion.11
  77.1 61.5 %reduce-scatter.2.cloned.1.call-done = f32[16,8,512]{2,0,1:T(8,128)} async-done(((f32[256,8,512]{2,0,1:T(8,128)}), f32[16,8,512]{2,0,1:T(8,128)}) %reduce-scatter.2.cloned.1.call-update) | async-done | bytes 262160 | tf_op jit(solution)/shard_map/reduce_scatter | solution.py:159
  140.2 3.4 collective-permute-start.2
  145.0 4.2 collective-permute-done.3
  150.0 3.4 reshape.554
  154.9 3.6 collective-permute-start.6
  159.8 2.2 convolution_bitcast_fusion.14
  169.7 1.6 convolution_bitcast_fusion.15
  177.2 1.6 convolution_bitcast_fusion.11
  181.4 8.9 %all-gather.5.cloned.1.call-done = bf16[256,10,512]{2,0,1:T(8,128)(2,1)} async-done(((bf16[16,10,512]{2,0,1:T(8,128)(2,1)}), bf16[256,10,512]{2,0,1:T(8,128)(2,1)}) %all-gather.5.cloned.1.call-update) | async-done | bytes 2621456 | tf_op jit(solution)/shard_map/all_gather | solution.py:100
  190.3 2.4 convolution_bitcast_fusion.10
  210.1 2.6 copy.37
  212.8 2.7 fusion.9
  216.7 253.1 %all-reduce.8.cloned.1.call-done = (f32[32,9,8,8]{0,1,3,2:T(8,128)}, f32[32,9,8,8]{0,1,3,2:T(8,128)}) async-done(((f32[32,9,8,8]{0,1,3,2:T(8,128)}, f32[32,9,8,8]{0,1,3,2:T(8,128)}), (f32[32,9,8,8]{0,1,3,2:T(8,128)}, f32[32,9,8,8]{0,1,3,2:T(8,128)})) %all-reduce.8.cloned.1.call-update) | async-done | bytes 147472 | tf_op jit(solution)/shard_map/psum | solution.py:169
  469.8 1.9 copy.64
  471.6 1.9 copy.65
  (153 shorter events, 51.4 us)
Async XLA Ops:
  7.2 62.7 %all-gather.3.cloned.1.call-start = ((), (), s32[]{:S(2)}) async-start(), calls=%async_computation.1 | async-start | bytes 2785280 | tf_op jit(solution)/shard_map/all_gather | solution.py:100
  8.2 5.3 %collective-permute-start = (bf16[16,1,512]{2,0,1:T(8,128)(2,1)S(1)}, bf16[16,1,512]{2,0,1:T(8,128)(2,1)S(1)}, u32[]{:S(2)}, u32[]{:S(2)}) collective-permute-start(bf16[16,1,512]{2,0,1:T(8,128)(2,1)S(1)} %get-tuple-element.26), channel_id=1, source_target_pairs={{0,1},{1,2},{2,3},{3,4},{4,5},{5,6},{6,7},{7,8},{8,9},{9,10},{10,1... | collective-permute-start | bytes 49160 | tf_op jit(solution)/shard_map/ppermute | solution.py:18
  12.0 5.6 %collective-permute-start.1 = (bf16[16,1,512]{2,0,1:T(8,128)(2,1)S(1)}, bf16[16,1,512]{2,0,1:T(8,128)(2,1)S(1)}, u32[]{:S(2)}, u32[]{:S(2)}) collective-permute-start(bf16[16,1,512]{2,0,1:T(8,128)(2,1)S(1)} %get-tuple-element.27), channel_id=1, source_target_pairs={{1,0},{2,1},{3,2},{4,3},{5,4},{6,5},{7,6},{8,7},{9,8},{10,9},{11,1... | collective-permute-start | bytes 49160 | tf_op jit(solution)/shard_map/ppermute | solution.py:19
  18.3 120.2 %reduce-scatter.2.cloned.1.call-start = ((), (), s32[]{:S(2)}) async-start(), calls=%async_computation.3 | async-start | bytes 4456448 | tf_op jit(solution)/shard_map/reduce_scatter | solution.py:159
  19.4 9.8 %collective-permute-start.4 = (bf16[16,1,512]{2,0,1:T(8,128)(2,1)S(1)}, bf16[16,1,512]{2,0,1:T(8,128)(2,1)S(1)}, u32[]{:S(2)}, u32[]{:S(2)}) collective-permute-start(bf16[16,1,512]{2,0,1:T(8,128)(2,1)S(1)} %get-tuple-element.28), channel_id=1, source_target_pairs={{0,1},{1,2},{2,3},{3,4},{4,5},{5,6},{6,7},{7,8},{8,9},{9,10},{10,1... | collective-permute-start | bytes 49160 | tf_op jit(solution)/shard_map/ppermute | solution.py:18
  23.2 6.7 %collective-permute-start.5 = (bf16[16,1,512]{2,0,1:T(8,128)(2,1)S(1)}, bf16[16,1,512]{2,0,1:T(8,128)(2,1)S(1)}, u32[]{:S(2)}, u32[]{:S(2)}) collective-permute-start(bf16[16,1,512]{2,0,1:T(8,128)(2,1)S(1)} %get-tuple-element.29), channel_id=1, source_target_pairs={{1,0},{2,1},{3,2},{4,3},{5,4},{6,5},{7,6},{8,7},{9,8},{10,9},{11,1... | collective-permute-start | bytes 49160 | tf_op jit(solution)/shard_map/ppermute | solution.py:19
  27.4 21.2 %copy-start.1 = (bf16[9,2,8,32,8]{4,3,2,1,0:T(8,128)(2,1)}, bf16[9,2,8,32,8]{4,3,2,1,0:T(8,128)(2,1)S(1)}, u32[]{:S(2)}) copy-start(bf16[9,2,8,32,8]{4,3,2,1,0:T(8,128)(2,1)S(1)} %copy.32) | copy-start | bytes 221188
  66.1 3.8 copy-start.12
  66.1 124.2 %all-gather.5.cloned.1.call-start = ((), (), s32[]{:S(2)}) async-start(), calls=%async_computation.2 | async-start | bytes 2785280 | tf_op jit(solution)/shard_map/all_gather | solution.py:100
  140.0 22.3 %copy-start.2 = (bf16[256,10,512]{2,0,1:T(8,128)(2,1)S(1)}, bf16[256,10,512]{2,0,1:T(8,128)(2,1)}, u32[]{:S(2)}) copy-start(bf16[256,10,512]{2,0,1:T(8,128)(2,1)} %all-gather.3.cloned.1.call-done) | copy-start | bytes 7864324
  140.2 4.9 %collective-permute-start.2 = (bf16[16,1,512]{2,0,1:T(8,128)(2,1)S(1)}, bf16[16,1,512]{2,0,1:T(8,128)(2,1)S(1)}, u32[]{:S(2)}, u32[]{:S(2)}) collective-permute-start(bf16[16,1,512]{2,0,1:T(8,128)(2,1)S(1)} %get-tuple-element.24), channel_id=1, source_target_pairs={{0,1},{1,2},{2,3},{3,4},{4,5},{5,6},{6,7},{7,8},{8,9},{9,10},{10,1... | collective-permute-start | bytes 49160 | tf_op jit(solution)/shard_map/ppermute | solution.py:18
  143.6 5.6 %collective-permute-start.3 = (bf16[16,1,512]{2,0,1:T(8,128)(2,1)S(1)}, bf16[16,1,512]{2,0,1:T(8,128)(2,1)S(1)}, u32[]{:S(2)}, u32[]{:S(2)}) collective-permute-start(bf16[16,1,512]{2,0,1:T(8,128)(2,1)S(1)} %get-tuple-element.25), channel_id=1, source_target_pairs={{1,0},{2,1},{3,2},{4,3},{5,4},{6,5},{7,6},{8,7},{9,8},{10,9},{11,1... | collective-permute-start | bytes 49160 | tf_op jit(solution)/shard_map/ppermute | solution.py:19
  149.9 319.8 %all-reduce.8.cloned.1.call-start = ((), (), s32[]{:S(2)}) async-start(), calls=%async_computation.4 | async-start | bytes 2097152 | tf_op jit(solution)/shard_map/psum | solution.py:169
  154.9 7.4 %collective-permute-start.6 = (bf16[16,1,512]{2,0,1:T(8,128)(2,1)S(1)}, bf16[16,1,512]{2,0,1:T(8,128)(2,1)S(1)}, u32[]{:S(2)}, u32[]{:S(2)}) collective-permute-start(bf16[16,1,512]{2,0,1:T(8,128)(2,1)S(1)} %get-tuple-element.22), channel_id=1, source_target_pairs={{0,1},{1,2},{2,3},{3,4},{4,5},{5,6},{6,7},{7,8},{8,9},{9,10},{10,1... | collective-permute-start | bytes 49160 | tf_op jit(solution)/shard_map/ppermute | solution.py:18
  158.5 6.0 %collective-permute-start.7 = (bf16[16,1,512]{2,0,1:T(8,128)(2,1)S(1)}, bf16[16,1,512]{2,0,1:T(8,128)(2,1)S(1)}, u32[]{:S(2)}, u32[]{:S(2)}) collective-permute-start(bf16[16,1,512]{2,0,1:T(8,128)(2,1)S(1)} %get-tuple-element.23), channel_id=1, source_target_pairs={{1,0},{2,1},{3,2},{4,3},{5,4},{6,5},{7,6},{8,7},{9,8},{10,9},{11,1... | collective-permute-start | bytes 49160 | tf_op jit(solution)/shard_map/ppermute | solution.py:19
  177.2 1.9 copy-start.8
  177.2 2.0 copy-start.7
  177.2 2.0 copy-start.9
  177.2 2.9 copy-start.14
  190.3 3.3 copy-start
  194.6 1.9 copy-start.3
  200.6 4.4 copy-start.6
  200.9 7.8 %copy-start.13 = (s32[64]{0:T(128)S(1)}, s32[64]{0:T(128)}, u32[]{:S(2)}) copy-start(s32[64]{0:T(128)} %fusion.114) | copy-start | bytes 772
  210.1 2.6 copy-start.5
  (3 other events, 2.2 us)
Sparse Core Ops, SparseCore 0:
  18.5 39.6 all-gather.2
  66.2 72.3 reduce-scatter.1
  150.1 40.1 all-gather.4
  210.2 259.4 all-reduce.7
where the time goes:
time: 481 us; the launch traced here: 480 us
  waiting for transfers between devices  334 us (69%)
  matrix products  48.1 us (10%)
  local copies, waits for them, and re-layouts  39.6 us (8%)
  other arithmetic  23 us (5%)
  starting transfers between devices  20.2 us (4%)
  between operations  15 us (3%)
    psum x1, waiting for transfers between devices, shards(): lax.psum((share_one, share_two), ('orient', 'strip'))  253 us
    reduce_scatter x1, waiting for transfers between devices, shards(): lax.psum_scatter(place_backward(mixed_taps, height, extent), 'orient', sc...  61.5 us
    dot_general x18, matrix products, weight_grad(): lax.dot_general(window, flat_center, (((1,), (1,)), ((), ())), preferred_...  19.6 us
    dot_general x1, matrix products, shards(): jnp.dot(rows_turned.reshape(9 * (local_width * lax.axis_size('orient')),...  18.7 us
    add x1, other arithmetic, place_backward(): summed + padded[tap_index, :, 2 - row_shift:2 - row_shift + height, 2 - c...  17.5 us
    ppermute x4, starting transfers between devices, with_halo(): before = lax.ppermute(last, axis, up)  14.7 us
    unnamed x51, local copies, waits for them, and re-layouts  12.8 us
    ppermute x4, waiting for transfers between devices, with_halo(): after = lax.ppermute(first, axis, down)  10.3 us
  transfers between devices with their start and end apart: 12, of which 9 were waited for; matrix products, arithmetic and copies ran while one was open for 17% of the time, Pallas kernels for 0%

commit v1 on v0

--- a/solution.py
+++ b/solution.py
@@ -97,7 +97,9 @@
     height, extent = (source.shape[1], source.shape[2])
     matrix = weights_row.reshape(tap_count * local_width, full_width)
     widened = with_halo(source, (("strip", 1),), 1)
-    gathered = lax.all_gather(widened, "orient", axis=0, tiled=True)
+    gathered = jnp.concatenate(
+        lax.all_to_all(jnp.stack([widened] * lax.axis_size("orient")), "orient", 0, 0), axis=0
+    )
     mixed_taps = jnp.dot(
         matrix, gathered.reshape(full_width, -1), preferred_element_type=jnp.float32
     )

time: 481 us -> 539 us (1.12); the launches traced: 480 us -> 530 us
  local copies, waits for them, and re-layouts: 39.6 us -> 68.8 us
  starting transfers between devices: 20.2 us -> 38.8 us
    all_to_all x0 -> x2, waiting for transfers between devices: none -> 66.1 us  [layer_forward(): lax.all_to_all(jnp.stack([widened] * lax.axis_size('orient')), 'orient',...]
    reduce_scatter x1, waiting for transfers between devices: 61.5 us -> 1.1 us  [shards(): lax.psum_scatter(place_backward(mixed_taps, height, extent), 'orient', sc...]
    all_to_all x0 -> x2, starting transfers between devices: none -> 14.8 us  [layer_forward(): lax.all_to_all(jnp.stack([widened] * lax.axis_size('orient')), 'orient',...]
    psum x1, waiting for transfers between devices: 253 us -> 263 us  [shards(): lax.psum((share_one, share_two), ('orient', 'strip'))]
    all_to_all x0 -> x4, local copies, waits for them, and re-layouts: none -> 9.7 us  [layer_forward(): lax.all_to_all(jnp.stack([widened] * lax.axis_size('orient')), 'orient',...]
    all_gather x2 -> x0, waiting for transfers between devices: 8.91 us -> none  [layer_forward(): gathered = lax.all_gather(widened, 'orient', axis=0, tiled=True)]
    another operation x38, local copies, waits for them, and re-layouts: 8.5 us -> 16.6 us  [weight_grad(): return jnp.stack(pieces, 0)]
    dot_general x0 -> x2, local copies, waits for them, and re-layouts: none -> 7.39 us  [layer_forward(): jnp.dot(matrix, gathered.reshape(full_width, -1), preferred_element_type=...]
  transfers between devices with their start and end apart: 12 -> 12, of which waited for: 9 -> 7; matrix products, arithmetic and copies ran while one was open for 17% -> 9% of each run, Pallas kernels for 0% -> 0%
where the time goes in v1:
time: 539 us; the launch traced here: 530 us
  waiting for transfers between devices  339 us (63%)
  local copies, waits for them, and re-layouts  68.8 us (13%)
  matrix products  47.6 us (9%)
  starting transfers between devices  38.8 us (7%)
  other arithmetic  19.7 us (4%)
  between operations  15.7 us (3%)
    psum x1, waiting for transfers between devices, shards(): lax.psum((share_one, share_two), ('orient', 'strip'))  263 us
    all_to_all x2, waiting for transfers between devices, layer_forward(): lax.all_to_all(jnp.stack([widened] * lax.axis_size('orient')), 'orient',...  66.1 us
    dot_general x18, matrix products, weight_grad(): lax.dot_general(window, flat_center, (((1,), (1,)), ((), ())), preferred_...  22.1 us
    ppermute x4, starting transfers between devices, with_halo(): before = lax.ppermute(last, axis, up)  18.6 us
    unnamed x58, local copies, waits for them, and re-layouts  18.4 us
    dot_general x1, matrix products, shards(): jnp.dot(rows_turned.reshape(9 * (local_width * lax.axis_size('orient')),...  18.3 us
    add x1, other arithmetic, place_backward(): summed + padded[tap_index, :, 2 - row_shift:2 - row_shift + height, 2 - c...  17.2 us
    another operation x38, local copies, waits for them, and re-layouts, weight_grad(): return jnp.stack(pieces, 0)  16.6 us
  transfers between devices with their start and end apart: 12, of which 7 were waited for; matrix products, arithmetic and copies ran while one was open for 9% of the time, Pallas kernels for 0%

profile of v1, /device:TPU:2, one launch (start us, length us, event | category | flops | bytes accessed | tf_op | source)
XLA Modules:
  0.0 530.0 jit_solution(9401786182140767617)
XLA Ops:
  8.2 3.8 collective-permute-start.4
  18.1 18.3 %fusion.56 = f32[9,256,10,512]{3,1,2,0:T(8,128)} fusion(bf16[9,16,256]{2,1,0:T(8,128)(2,1)S(1)} %convert_element_type.51, bf16[10,2,8,512]{3,2,1,0:T(8,128)(2,1)S(1)} %get-tuple-element.21), kind=kOutput, calls=%fused_computation.108 | convolution fusion | flops 377487360 | bytes 47423488 | tf_op jit(solution)/shard_map/dot_general | solution.py:155
  36.4 17.2 %fusion.8 = f32[256,8,512]{2,0,1:T(8,128)} fusion(f32[9,256,10,512]{3,1,2,0:T(8,128)} %fusion.56), kind=kLoop, calls=%fused_computation.26 | loop fusion | flops 8388608 | bytes 63963136 | tf_op jit(solution)/shard_map/add | solution.py:84
  54.6 4.5 collective-permute-start
  60.6 4.2 collective-permute-done.1
  66.6 6.6 %all-to-all-start = ((bf16[16,16,10,512]{3,1,2,0:T(8,128)(2,1)}), bf16[16,16,10,512]{3,1,2,0:T(8,128)(2,1)S(1)}, u32[]{:S(2)}, u32[]{:S(2)}) async-start(bf16[16,16,10,512]{3,1,2,0:T(8,128)(2,1)} %stack.44), calls=%async_computation | async-start | bytes 5242880 | tf_op jit(solution)/shard_map/all_to_all | solution.py:101
  73.3 2.8 reshape.558
  77.3 2.4 copy.38
  79.6 2.8 reshape.556
  82.8 47.4 %all-to-all-done = bf16[16,16,10,512]{3,1,2,0:T(8,128)(2,1)S(1)} async-done(((bf16[16,16,10,512]{3,1,2,0:T(8,128)(2,1)}), bf16[16,16,10,512]{3,1,2,0:T(8,128)(2,1)S(1)}, u32[]{:S(2)}, u32[]{:S(2)}) %all-to-all-start) | async-done | bytes 2621472 | tf_op jit(solution)/shard_map/all_to_all | solution.py:101
  132.3 4.2 copy.85
  136.5 4.4 copy.43
  148.0 4.7 collective-permute-start.2
  154.0 5.6 %collective-permute-start.6 = (bf16[16,1,512]{2,0,1:T(8,128)(2,1)S(1)}, bf16[16,1,512]{2,0,1:T(8,128)(2,1)S(1)}, u32[]{:S(2)}, u32[]{:S(2)}) collective-permute-start(bf16[16,1,512]{2,0,1:T(8,128)(2,1)S(1)} %get-tuple-element.22), channel_id=1, source_target_pairs={{0,1},{1,2},{2,3},{3,4},{4,5},{5,6},{6,7},{7,8},{8,9},{9,10},{10,1... | collective-permute-start | bytes 49160 | tf_op jit(solution)/shard_map/ppermute | solution.py:18
  161.9 4.5 collective-permute-done.7
  169.8 8.2 %all-to-all-start.1 = ((bf16[16,16,10,512]{3,1,2,0:T(8,128)(2,1)}), bf16[16,16,10,512]{3,1,2,0:T(8,128)(2,1)}, u32[]{:S(2)}, u32[]{:S(2)}) async-start(bf16[16,16,10,512]{3,1,2,0:T(8,128)(2,1)} %stack.45), calls=%async_computation.1 | async-start | bytes 5242880 | tf_op jit(solution)/shard_map/all_to_all | solution.py:101
  191.7 18.6 %all-to-all-done.1 = bf16[16,16,10,512]{3,1,2,0:T(8,128)(2,1)} async-done(((bf16[16,16,10,512]{3,1,2,0:T(8,128)(2,1)}), bf16[16,16,10,512]{3,1,2,0:T(8,128)(2,1)}, u32[]{:S(2)}, u32[]{:S(2)}) %all-to-all-start.1) | async-done | bytes 2621472 | tf_op jit(solution)/shard_map/all_to_all | solution.py:101
  210.3 2.1 copy.61
  222.4 2.2 convolution_bitcast_fusion.2
  234.4 2.2 convolution_bitcast_fusion
  241.2 3.8 copy.44
  245.0 4.4 copy.86
  249.4 3.0 copy.45
  255.9 263.3 %all-reduce.8.cloned.1.call-done = (f32[32,9,8,8]{0,1,3,2:T(8,128)}, f32[32,9,8,8]{0,1,3,2:T(8,128)}) async-done(((f32[32,9,8,8]{0,1,3,2:T(8,128)}, f32[32,9,8,8]{0,1,3,2:T(8,128)}), (f32[32,9,8,8]{0,1,3,2:T(8,128)}, f32[32,9,8,8]{0,1,3,2:T(8,128)})) %all-reduce.8.cloned.1.call-update) | async-done | bytes 147472 | tf_op jit(solution)/shard_map/psum | solution.py:171
  (165 shorter events, 73.1 us)
Async XLA Ops:
  7.2 138.5 %reduce-scatter.2.cloned.1.call-start = ((), (), s32[]{:S(2)}) async-start(), calls=%async_computation.3 | async-start | bytes 4456448 | tf_op jit(solution)/shard_map/reduce_scatter | solution.py:161
  8.2 28.2 %copy-start.4 = (bf16[2,8,8,512]{3,1,0,2:T(8,128)(2,1)}, bf16[2,8,8,512]{3,1,0,2:T(8,128)(2,1)S(1)}, u32[]{:S(2)}) copy-start(bf16[2,8,8,512]{3,1,0,2:T(8,128)(2,1)S(1)} %copy.108) | copy-start | bytes 393220
  8.2 9.8 %collective-permute-start.4 = (bf16[16,1,512]{2,0,1:T(8,128)(2,1)S(1)}, bf16[16,1,512]{2,0,1:T(8,128)(2,1)S(1)}, u32[]{:S(2)}, u32[]{:S(2)}) collective-permute-start(bf16[16,1,512]{2,0,1:T(8,128)(2,1)S(1)} %get-tuple-element.28), channel_id=1, source_target_pairs={{0,1},{1,2},{2,3},{3,4},{4,5},{5,6},{6,7},{7,8},{8,9},{9,10},{10,1... | collective-permute-start | bytes 49160 | tf_op jit(solution)/shard_map/ppermute | solution.py:18
  12.0 6.0 %collective-permute-start.5 = (bf16[16,1,512]{2,0,1:T(8,128)(2,1)S(1)}, bf16[16,1,512]{2,0,1:T(8,128)(2,1)S(1)}, u32[]{:S(2)}, u32[]{:S(2)}) collective-permute-start(bf16[16,1,512]{2,0,1:T(8,128)(2,1)S(1)} %get-tuple-element.29), channel_id=1, source_target_pairs={{1,0},{2,1},{3,2},{4,3},{5,4},{6,5},{7,6},{8,7},{9,8},{10,9},{11,1... | collective-permute-start | bytes 49160 | tf_op jit(solution)/shard_map/ppermute | solution.py:19
  16.2 20.2 %copy-start = (bf16[9,2,8,32,8]{4,3,2,1,0:T(8,128)(2,1)}, bf16[9,2,8,32,8]{4,3,2,1,0:T(8,128)(2,1)S(1)}, u32[]{:S(2)}) copy-start(bf16[9,2,8,32,8]{4,3,2,1,0:T(8,128)(2,1)S(1)} %copy.36) | copy-start | bytes 221188
  18.0 18.4 %copy-start.15 = (bf16[16,1,512]{2,0,1:T(8,128)(2,1)}, bf16[16,1,512]{2,0,1:T(8,128)(2,1)S(1)}, u32[]{:S(2)}) copy-start(bf16[16,1,512]{2,0,1:T(8,128)(2,1)S(1)} %collective-permute-done.4) | copy-start | bytes 49156
  18.0 18.4 %copy-start.16 = (bf16[16,1,512]{2,0,1:T(8,128)(2,1)}, bf16[16,1,512]{2,0,1:T(8,128)(2,1)S(1)}, u32[]{:S(2)}) copy-start(bf16[16,1,512]{2,0,1:T(8,128)(2,1)S(1)} %collective-permute-done.5) | copy-start | bytes 49156
  54.6 6.0 %collective-permute-start = (bf16[16,1,512]{2,0,1:T(8,128)(2,1)S(1)}, bf16[16,1,512]{2,0,1:T(8,128)(2,1)S(1)}, u32[]{:S(2)}, u32[]{:S(2)}) collective-permute-start(bf16[16,1,512]{2,0,1:T(8,128)(2,1)S(1)} %get-tuple-element.26), channel_id=1, source_target_pairs={{0,1},{1,2},{2,3},{3,4},{4,5},{5,6},{6,7},{7,8},{8,9},{9,10},{10,1... | collective-permute-start | bytes 49160 | tf_op jit(solution)/shard_map/ppermute | solution.py:18
  59.1 5.6 %collective-permute-start.1 = (bf16[16,1,512]{2,0,1:T(8,128)(2,1)S(1)}, bf16[16,1,512]{2,0,1:T(8,128)(2,1)S(1)}, u32[]{:S(2)}, u32[]{:S(2)}) collective-permute-start(bf16[16,1,512]{2,0,1:T(8,128)(2,1)S(1)} %get-tuple-element.27), channel_id=1, source_target_pairs={{1,0},{2,1},{3,2},{4,3},{5,4},{6,5},{7,6},{8,7},{9,8},{10,9},{11,1... | collective-permute-start | bytes 49160 | tf_op jit(solution)/shard_map/ppermute | solution.py:19
  66.6 9.5 %copy-start.6 = (bf16[32,9,8,8]{0,3,2,1:T(8,128)(2,1)S(1)}, bf16[32,9,8,8]{0,3,2,1:T(8,128)(2,1)}, u32[]{:S(2)}) copy-start(bf16[32,9,8,8]{0,3,2,1:T(8,128)(2,1)} %param.7) | copy-start | bytes 110596
  66.6 63.6 %all-to-all-start = ((bf16[16,16,10,512]{3,1,2,0:T(8,128)(2,1)}), bf16[16,16,10,512]{3,1,2,0:T(8,128)(2,1)S(1)}, u32[]{:S(2)}, u32[]{:S(2)}) async-start(bf16[16,16,10,512]{3,1,2,0:T(8,128)(2,1)} %stack.44), calls=%async_computation | async-start | bytes 5242880 | tf_op jit(solution)/shard_map/all_to_all | solution.py:101
  73.2 9.5 %copy-start.17 = (s32[8,512]{1,0:T(8,128)S(1)}, s32[8,512]{1,0:T(8,128)}, u32[]{:S(2)}) copy-start(s32[8,512]{1,0:T(8,128)} %param.9) | copy-start | bytes 49156
  145.7 15.2 %copy-start.2 = (bf16[16,16,10,512]{3,1,0,2:T(8,128)(2,1)S(1)}, bf16[16,16,10,512]{3,1,0,2:T(8,128)(2,1)}, u32[]{:S(2)}) copy-start(bf16[16,16,10,512]{3,1,0,2:T(8,128)(2,1)} %copy.49) | copy-start | bytes 7864324
  147.3 19.2 %copy-start.3 = (bf16[16,16,10,512]{3,1,0,2:T(8,128)(2,1)S(1)}, bf16[16,16,10,512]{3,1,0,2:T(8,128)(2,1)}, u32[]{:S(2)}) copy-start(bf16[16,16,10,512]{3,1,0,2:T(8,128)(2,1)} %copy.49) | copy-start | bytes 7864324
  148.0 19.9 %collective-permute-start.2 = (bf16[16,1,512]{2,0,1:T(8,128)(2,1)}, bf16[16,1,512]{2,0,1:T(8,128)(2,1)S(1)}, u32[]{:S(2)}, u32[]{:S(2)}) collective-permute-start(bf16[16,1,512]{2,0,1:T(8,128)(2,1)} %get-tuple-element.24), channel_id=1, source_target_pairs={{0,1},{1,2},{2,3},{3,4},{4,5},{5,6},{6,7},{7,8},{8,9},{9,10},{10,1... | collective-permute-start | bytes 49160 | tf_op jit(solution)/shard_map/ppermute | solution.py:18
  152.7 15.2 %collective-permute-start.3 = (bf16[16,1,512]{2,0,1:T(8,128)(2,1)}, bf16[16,1,512]{2,0,1:T(8,128)(2,1)S(1)}, u32[]{:S(2)}, u32[]{:S(2)}) collective-permute-start(bf16[16,1,512]{2,0,1:T(8,128)(2,1)} %get-tuple-element.25), channel_id=1, source_target_pairs={{1,0},{2,1},{3,2},{4,3},{5,4},{6,5},{7,6},{8,7},{9,8},{10,9},{11,1... | collective-permute-start | bytes 49160 | tf_op jit(solution)/shard_map/ppermute | solution.py:19
  154.0 7.9 %collective-permute-start.6 = (bf16[16,1,512]{2,0,1:T(8,128)(2,1)S(1)}, bf16[16,1,512]{2,0,1:T(8,128)(2,1)S(1)}, u32[]{:S(2)}, u32[]{:S(2)}) collective-permute-start(bf16[16,1,512]{2,0,1:T(8,128)(2,1)S(1)} %get-tuple-element.22), channel_id=1, source_target_pairs={{0,1},{1,2},{2,3},{3,4},{4,5},{5,6},{6,7},{7,8},{8,9},{9,10},{10,1... | collective-permute-start | bytes 49160 | tf_op jit(solution)/shard_map/ppermute | solution.py:18
  159.6 6.8 %collective-permute-start.7 = (bf16[16,1,512]{2,0,1:T(8,128)(2,1)S(1)}, bf16[16,1,512]{2,0,1:T(8,128)(2,1)S(1)}, u32[]{:S(2)}, u32[]{:S(2)}) collective-permute-start(bf16[16,1,512]{2,0,1:T(8,128)(2,1)S(1)} %get-tuple-element.23), channel_id=1, source_target_pairs={{1,0},{2,1},{3,2},{4,3},{5,4},{6,5},{7,6},{8,7},{9,8},{10,9},{11,1... | collective-permute-start | bytes 49160 | tf_op jit(solution)/shard_map/ppermute | solution.py:19
  169.8 40.5 %all-to-all-start.1 = ((bf16[16,16,10,512]{3,1,2,0:T(8,128)(2,1)}), bf16[16,16,10,512]{3,1,2,0:T(8,128)(2,1)}, u32[]{:S(2)}, u32[]{:S(2)}) async-start(bf16[16,16,10,512]{3,1,2,0:T(8,128)(2,1)} %stack.45), calls=%async_computation.1 | async-start | bytes 5242880 | tf_op jit(solution)/shard_map/all_to_all | solution.py:101
  177.9 341.3 %all-reduce.8.cloned.1.call-start = ((), (), s32[]{:S(2)}) async-start(), calls=%async_computation.4 | async-start | bytes 2097152 | tf_op jit(solution)/shard_map/psum | solution.py:171
  234.4 4.2 copy-start.7
  234.4 4.2 copy-start.8
  234.4 4.3 copy-start.9
  234.4 4.3 copy-start.10
  (6 other events, 11.4 us)
Sparse Core Ops, SparseCore 0:
  53.8 91.8 reduce-scatter.1
  253.8 265.3 all-reduce.7
